TPU v7x, 512 devices: a whole 4x8x8 slice. The times are simulated.
512 devices in a mesh: ep: 128 (over y, z, core), dp: 4 (over x).
Axes of the slice: x: 4, y: 8, z: 8, core: 2. Of those that a mesh axis runs over, the one named last changes fastest.
Arguments:
- tokens: bfloat16 [2, 2048, 3584], P(None, ('ep', 'dp')), may hold values from -6 to 6
- routing: int32 [2, 2048, 8], P(None, 'ep'), may hold values from 0 to 127, all different within a row; in each aligned block of 16 rows (0 to 15, 16 to 31, ..., all dimensions but the last counted through in order) at most 2 rows name the same one
- gate_values: float32 [2, 2048, 8], P(None, 'ep'), may hold values from 0.05 to 0.5
- held_weight: bfloat16 [128, 3584, 1024], P('ep', None, 'dp'), may hold values from -0.09375 to 0.09375
- scale_table: float32 [128, 28, 8], P(None, None, 'dp'), may hold values from 0.25 to 4
- old_expert: int32 [128], replicated, may hold values from 0 to 127, as said below
- new_expert: int32 [128], replicated, may hold values from 0 to 127, as said below
Outputs:
- combined: bfloat16 [2, 2048, 1024], P(None, 'ep', 'dp')
- moved_weight: bfloat16 [128, 3584, 1024], P('ep', None, 'dp')
Inputs may be any that keep to these rules, and one draw needn't show every extreme that they name: `routing`: each row names 8 different experts; in each aligned block of 16 token rows of a step no expert is named by more than 2 rows. `old_expert`: A permutation of the experts over the slots. `new_expert`: A permutation of the experts over the slots; it equals old_expert except at exactly 32 slots, whose experts are permuted among themselves so that each of them changes.
All inputs are finite; a program needn't handle non-finite values.
Results may differ from a plain program's by a relative error of at most 0.0039.
Values may be sent and summed in bfloat16 or wider, within the bound.
No kernel may reach another device: no remote copies, remote signals or barrier semaphores. Data moves between devices by JAX's collectives and lax.ppermute only.
A program may use at most 64 MiB of HBM per device.

v0:
```python
import jax
import jax.numpy as jnp
from jax import lax
from jax.sharding import PartitionSpec as P


def inverse_place(expert_at):
    count = expert_at.shape[0]
    labels = jnp.arange(count, dtype=jnp.int32)
    match = expert_at[None, :] == labels[:, None]
    return jnp.sum(jnp.where(match, labels[None, :], 0), axis=1)


def source_slots(old_expert, new_expert):
    labels = jnp.arange(old_expert.shape[0], dtype=jnp.int32)
    match = old_expert[None, :] == new_expert[:, None]
    return jnp.sum(jnp.where(match, labels[None, :], 0), axis=1)


def scaled_product(token_rows, weight_block, scales):
    row_blocks = scales.shape[0]
    block_rows = weight_block.shape[0] // row_blocks
    partial_value = jnp.einsum(
        "rbi,bif->rbf",
        token_rows.reshape(token_rows.shape[0], row_blocks, block_rows),
        weight_block.reshape(row_blocks, block_rows, weight_block.shape[1]),
        preferred_element_type=jnp.float32,
    )
    widened = jnp.repeat(scales, weight_block.shape[1] // scales.shape[1], axis=1)
    return jnp.sum(partial_value * widened[None, :, :], axis=1)


def expert_service(weight_block, scales):

    def serve_rows(arrived):

        def one_slot(slot_rows):
            return jax.nn.silu(scaled_product(slot_rows, weight_block, scales)).astype(jnp.bfloat16)

        activated = lax.map(one_slot, arrived)
        return lax.all_to_all(activated, "ep", split_axis=1, concat_axis=1, tiled=True)

    return serve_rows


def route_pairs(routing, expert_at, peers):
    pair_ids = routing.reshape(-1)
    labels = jnp.arange(peers, dtype=jnp.int32)
    onehot = (pair_ids[:, None] == labels[None, :]).astype(jnp.int32)
    before = jnp.cumsum(onehot, axis=0) - onehot
    slot_rank = jnp.sum(before * onehot, axis=1)
    owners = jnp.sum(onehot * inverse_place(expert_at)[None, :], axis=1)
    return slot_rank * peers + owners


def shards(tokens, routing, gate_values, held_weight, scale_table, old_expert, new_expert):
    peers = lax.axis_size("ep")
    my_slot = lax.axis_index("ep")
    group_size = routing.shape[1]
    top_count = routing.shape[2]
    capacity = min(group_size, max(2, 2 * group_size * top_count // peers))
    hidden_width = held_weight.shape[2]
    old_block = held_weight[0]
    sources = source_slots(old_expert, new_expert)
    pieces = old_block.reshape(peers, old_block.shape[0] // peers, hidden_width)
    new_block = lax.all_to_all(
        jnp.take(
            lax.all_to_all(pieces, "ep", split_axis=0, concat_axis=0, tiled=True), sources, axis=0
        ),
        "ep",
        split_axis=0,
        concat_axis=0,
        tiled=True,
    ).reshape(old_block.shape)
    first_serve = (new_block, new_expert)
    serve_plans = [first_serve] + [(new_block, new_expert)] * (tokens.shape[0] - 1)
    grouped = lax.all_gather(tokens, "dp", axis=1, tiled=True)
    columns = grouped.shape[2]
    combined_steps = []
    for decode_step in range(tokens.shape[0]):
        weight_block, expert_at = serve_plans[decode_step]
        scales = scale_table[expert_at[my_slot]]
        target = route_pairs(routing[decode_step], expert_at, peers)
        repeated = jnp.repeat(grouped[decode_step], top_count, axis=0)
        send_buffer = jnp.zeros((capacity * peers, columns), grouped.dtype).at[target].set(repeated)
        send_buffer = send_buffer.reshape(capacity, peers, columns)
        serve_rows = expert_service(weight_block, scales)
        returned = serve_rows(
            lax.all_to_all(send_buffer, "ep", split_axis=1, concat_axis=1, tiled=True)
        )
        activated = returned.reshape(capacity * peers, hidden_width)[target].astype(jnp.float32)
        activated = activated.reshape(group_size, top_count, hidden_width)
        weighted = jnp.sum(gate_values[decode_step][:, :, None] * activated, axis=1)
        combined_steps.append(weighted.astype(jnp.bfloat16))
    return (jnp.stack(combined_steps), new_block[None])


def solution(mesh):
    placed = (
        P(None, ("ep", "dp"), None),
        P(None, "ep", None),
        P(None, "ep", None),
        P("ep", None, "dp"),
        P(None, None, "dp"),
        P(),
        P(),
    )
    return jax.shard_map(
        shards,
        mesh=mesh,
        in_specs=placed,
        out_specs=(P(None, "ep", "dp"), P("ep", None, "dp")),
        check_vma=False,
    )
```

profile of v0, /device:TPU:1, one launch (start us, length us, event | category | flops | bytes accessed | tf_op | source)
XLA Modules:
  0.0 315.5 jit_solution(4355905081281846887)
XLA Ops:
  3.1 10.5 %all_gather.3 = bf16[2,16,3584]{2,0,1:T(2,128)(2,1)S(1)} all-gather(bf16[2,4,3584]{2,0,1:T(2,128)(2,1)S(1)} %copy.58), channel_id=1, replica_groups=mesh['ep'=128,'dp'=4] {'dp'}, dimensions={1}, use_global_device_ids=true | all-gather | bytes 286720 | tf_op jit(solution)/shard_map/all_gather | solution.py:77
  17.5 3.1 copy.60
  20.7 20.5 %all-to-all-start = ((bf16[2,128,3584]{2,0,1:T(2,128)(2,1)}), bf16[2,128,3584]{2,0,1:T(2,128)(2,1)S(1)}, u32[]{:S(2)}, u32[]{:S(2)}) async-start(bf16[2,128,3584]{2,0,1:T(2,128)(2,1)} %copy.60), calls=%async_computation | async-start | bytes 3670016 | tf_op jit(solution)/shard_map/all_to_all | solution.py:89
  41.1 3.7 %reshape_squeeze.3 = bf16[128,28,256]{2,1,0:T(8,128)(2,1)} reshape(bf16[1,3584,256]{2,1,0:T(8,128)(2,1)} %param.14) | data formatting | bytes 3670016 | tf_op jit(solution)/shard_map/reshape;squeeze | solution.py:65
  44.9 42.7 %all-to-all-done = bf16[2,128,3584]{2,0,1:T(2,128)(2,1)S(1)} async-done(((bf16[2,128,3584]{2,0,1:T(2,128)(2,1)}), bf16[2,128,3584]{2,0,1:T(2,128)(2,1)S(1)}, u32[]{:S(2)}, u32[]{:S(2)}) %all-to-all-start) | async-done | bytes 1835040 | tf_op jit(solution)/shard_map/all_to_all | solution.py:89
  88.9 7.8 %all-to-all-start.1 = ((bf16[128,28,256]{2,1,0:T(8,128)(2,1)}), bf16[128,28,256]{2,1,0:T(8,128)(2,1)S(1)}, u32[]{:S(2)}, u32[]{:S(2)}) async-start(bf16[128,28,256]{2,1,0:T(8,128)(2,1)} %reshape_squeeze.3), calls=%async_computation.1 | async-start | bytes 4194304 | tf_op jit(solution)/shard_map/all_to_all | solution.py:68
  96.7 3.3 %scatter_custom_fusion.1 = bf16[256,3584]{1,0:T(8,128)(2,1)} fusion(s32[128]{0:T(128)S(1)} %get-tuple-element.141, bf16[]{:T(256)} %constant.58.clone.1, bf16[16,3584]{1,0:T(8,128)(2,1)S(1)} %get-tuple-element.142), kind=kCustom, calls=%fused_computation.24 | custom fusion | bytes 1949698 | tf_op jit(solution)/shard_map/scatter | solution.py:85
  100.0 4.6 %copy.69 = bf16[2,128,3584]{2,0,1:T(2,128)(2,1)} copy(bf16[2,128,3584]{2,1,0:T(8,128)(2,1)} %bitcast.125) | data formatting | bytes 3670016 | tf_op jit(solution)/shard_map/reshape | solution.py:86
  104.6 44.2 %all-to-all-done.1 = bf16[128,28,256]{2,1,0:T(8,128)(2,1)S(1)} async-done(((bf16[128,28,256]{2,1,0:T(8,128)(2,1)}), bf16[128,28,256]{2,1,0:T(8,128)(2,1)S(1)}, u32[]{:S(2)}, u32[]{:S(2)}) %all-to-all-start.1) | async-done | bytes 1835040 | tf_op jit(solution)/shard_map/all_to_all | solution.py:68
  148.8 8.1 %all-to-all-start.4 = ((bf16[2,128,3584]{2,0,1:T(2,128)(2,1)}), bf16[2,128,3584]{2,0,1:T(2,128)(2,1)}, u32[]{:S(2)}, u32[]{:S(2)}) async-start(bf16[2,128,3584]{2,0,1:T(2,128)(2,1)} %copy.69), calls=%async_computation.4 | async-start | bytes 3670016 | tf_op jit(solution)/shard_map/all_to_all | solution.py:89
  159.0 3.2 %broadcast_select_fusion = bf16[128,28,256]{2,1,0:T(8,128)(2,1)} fusion(bf16[128,28,256]{2,1,0:T(8,128)(2,1)} %gather_fusion, pred[128]{0:T(512)(128)(4,1)S(1)} %compare_and_fusion), kind=kLoop, calls=%fused_computation.23 | loop fusion | flops 917504 | bytes 3670144 | tf_op jit(solution)/shard_map/jit(_take)/select_n | solution.py:67
  162.2 40.9 %all-to-all-done.4 = bf16[2,128,3584]{2,0,1:T(2,128)(2,1)} async-done(((bf16[2,128,3584]{2,0,1:T(2,128)(2,1)}), bf16[2,128,3584]{2,0,1:T(2,128)(2,1)}, u32[]{:S(2)}, u32[]{:S(2)}) %all-to-all-start.4) | async-done | bytes 1835040 | tf_op jit(solution)/shard_map/all_to_all | solution.py:89
  203.1 7.8 %all-to-all-start.2 = ((bf16[128,28,256]{2,1,0:T(8,128)(2,1)}), bf16[128,28,256]{2,1,0:T(8,128)(2,1)S(1)}, u32[]{:S(2)}, u32[]{:S(2)}) async-start(bf16[128,28,256]{2,1,0:T(8,128)(2,1)} %broadcast_select_fusion), calls=%async_computation.2 | async-start | bytes 4194304 | tf_op jit(solution)/shard_map/all_to_all | solution.py:66
  213.8 5.6 %copy.62 = bf16[2,128,3584]{1,2,0:T(8,128)(2,1)} copy(bf16[2,128,3584]{2,0,1:T(2,128)(2,1)} %copy-done.3) | data formatting | bytes 3670016 | tf_op jit(solution)/shard_map/while | solution.py:40
  219.3 5.5 %copy.70 = bf16[2,128,3584]{1,2,0:T(8,128)(2,1)} copy(bf16[2,128,3584]{2,0,1:T(2,128)(2,1)} %all-to-all-done.4) | data formatting | bytes 3670016 | tf_op jit(solution)/shard_map/while | solution.py:40
  224.9 38.2 %all-to-all-done.2 = bf16[128,28,256]{2,1,0:T(8,128)(2,1)S(1)} async-done(((bf16[128,28,256]{2,1,0:T(8,128)(2,1)}), bf16[128,28,256]{2,1,0:T(8,128)(2,1)S(1)}, u32[]{:S(2)}, u32[]{:S(2)}) %all-to-all-start.2) | async-done | bytes 1835040 | tf_op jit(solution)/shard_map/all_to_all | solution.py:66
  265.0 5.2 %while.22 = (s32[]{:T(128)}, bf16[2,128,256]{2,1,0:T(8,128)(2,1)S(1)}, bf16[2,128,3584]{1,2,0:T(8,128)(2,1)}, bf16[128,28,256]{2,1,0:T(8,128)(2,1)}, f32[28,2]{1...) while((s32[]{:T(128)}, bf16[2,128,256]{2,1,0:T(8,128)(2,1)S(1)}, ...), condition=%wide.wide.region_8.9_spmd, body=%wide.wide.region_6.8_spmd.sunk | while | flops 236847104 | bytes 12439901 | solution.py:40
  270.9 7.7 %all-to-all-start.3 = ((bf16[2,128,256]{2,0,1:T(2,128)(2,1)}), bf16[2,128,256]{2,0,1:T(2,128)(2,1)S(1)}, u32[]{:S(2)}, u32[]{:S(2)}) async-start(bf16[2,128,256]{2,0,1:T(2,128)(2,1)} %copy.64), calls=%async_computation.3 | async-start | bytes 262144 | tf_op jit(solution)/shard_map/all_to_all | solution.py:41
  278.7 3.9 %reshape_reshape.8 = bf16[28,128,256]{2,1,0:T(8,128)(2,1)} reshape(bf16[128,28,256]{2,1,0:T(8,128)(2,1)} %get-tuple-element.307) | data formatting | bytes 3670016 | tf_op jit(solution)/shard_map/while/body/eval_jaxpr/reshape;reshape | solution.py:26
  282.6 4.6 %while.23 = (s32[]{:T(128)}, bf16[2,128,256]{2,1,0:T(8,128)(2,1)S(1)}, bf16[2,128,3584]{1,2,0:T(8,128)(2,1)S(1)}, bf16[128,28,256]{2,1,0:T(8,128)(2,1)}, f32[28,...) while((s32[]{:T(128)}, bf16[2,128,256]{2,1,0:T(8,128)(2,1)S(1)}, ...), condition=%wide.wide.region_16.17_spmd, body=%wide.wide.region_14.16_spmd.sunk | while | flops 236847104 | bytes 12439901 | solution.py:40
  288.0 3.0 all-to-all-done.3
  290.9 10.8 %all-to-all-start.5 = ((bf16[2,128,256]{2,0,1:T(2,128)(2,1)}), bf16[2,128,256]{2,0,1:T(2,128)(2,1)S(1)}, u32[]{:S(2)}, u32[]{:S(2)}) async-start(bf16[2,128,256]{2,0,1:T(2,128)(2,1)} %copy.72), calls=%async_computation.5 | async-start | bytes 262144 | tf_op jit(solution)/shard_map/all_to_all | solution.py:41
  301.9 3.7 %broadcast_in_dim_reshape.3 = bf16[1,3584,256]{2,1,0:T(8,128)(2,1)} reshape(bf16[128,28,256]{2,1,0:T(8,128)(2,1)} %get-tuple-element.308) | data formatting | bytes 3670016 | tf_op jit(solution)/shard_map/broadcast_in_dim;reshape | solution.py:95
  306.6 7.3 %all-to-all-done.5 = bf16[2,128,256]{2,0,1:T(2,128)(2,1)S(1)} async-done(((bf16[2,128,256]{2,0,1:T(2,128)(2,1)}), bf16[2,128,256]{2,0,1:T(2,128)(2,1)S(1)}, u32[]{:S(2)}, u32[]{:S(2)}) %all-to-all-start.5) | async-done | bytes 131104 | tf_op jit(solution)/shard_map/all_to_all | solution.py:41
  (85 shorter events, 26.3 us)
Async XLA Ops:
  0.6 212.8 %copy-start = (f32[128,28,2]{0,2,1:T(2,128)S(1)}, f32[128,28,2]{0,2,1:T(2,128)}, u32[]{:S(2)}) copy-start(f32[128,28,2]{0,2,1:T(2,128)} %param.15) | copy-start | bytes 86020
  20.7 67.0 %all-to-all-start = ((bf16[2,128,3584]{2,0,1:T(2,128)(2,1)}), bf16[2,128,3584]{2,0,1:T(2,128)(2,1)S(1)}, u32[]{:S(2)}, u32[]{:S(2)}) async-start(bf16[2,128,3584]{2,0,1:T(2,128)(2,1)} %copy.60), calls=%async_computation | async-start | bytes 3670016 | tf_op jit(solution)/shard_map/all_to_all | solution.py:89
  87.6 1.3 copy-start.3
  88.9 59.9 %all-to-all-start.1 = ((bf16[128,28,256]{2,1,0:T(8,128)(2,1)}), bf16[128,28,256]{2,1,0:T(8,128)(2,1)S(1)}, u32[]{:S(2)}, u32[]{:S(2)}) async-start(bf16[128,28,256]{2,1,0:T(8,128)(2,1)} %reshape_squeeze.3), calls=%async_computation.1 | async-start | bytes 4194304 | tf_op jit(solution)/shard_map/all_to_all | solution.py:68
  148.8 54.3 %all-to-all-start.4 = ((bf16[2,128,3584]{2,0,1:T(2,128)(2,1)}), bf16[2,128,3584]{2,0,1:T(2,128)(2,1)}, u32[]{:S(2)}, u32[]{:S(2)}) async-start(bf16[2,128,3584]{2,0,1:T(2,128)(2,1)} %copy.69), calls=%async_computation.4 | async-start | bytes 3670016 | tf_op jit(solution)/shard_map/all_to_all | solution.py:89
  162.2 48.7 %copy-start.7 = (s32[128]{0:T(128)S(1)}, s32[128]{0:T(128)}, u32[]{:S(2)}) copy-start(s32[128]{0:T(128)} %param.17) | copy-start | bytes 1540
  162.2 51.5 %copy-start.6 = (f32[2,16,8]{1,2,0:T(8,128)S(1)}, f32[2,16,8]{1,2,0:T(8,128)}, u32[]{:S(2)}) copy-start(f32[2,16,8]{1,2,0:T(8,128)} %param.13) | copy-start | bytes 3076
  203.1 59.9 %all-to-all-start.2 = ((bf16[128,28,256]{2,1,0:T(8,128)(2,1)}), bf16[128,28,256]{2,1,0:T(8,128)(2,1)S(1)}, u32[]{:S(2)}, u32[]{:S(2)}) async-start(bf16[128,28,256]{2,1,0:T(8,128)(2,1)} %broadcast_select_fusion), calls=%async_computation.2 | async-start | bytes 4194304 | tf_op jit(solution)/shard_map/all_to_all | solution.py:66
  263.1 1.9 copy-start.1
  265.0 1.8 copy-start.5
  267.6 1.8 copy-start.5
  270.9 20.0 %all-to-all-start.3 = ((bf16[2,128,256]{2,0,1:T(2,128)(2,1)}), bf16[2,128,256]{2,0,1:T(2,128)(2,1)S(1)}, u32[]{:S(2)}, u32[]{:S(2)}) async-start(bf16[2,128,256]{2,0,1:T(2,128)(2,1)} %copy.64), calls=%async_computation.3 | async-start | bytes 262144 | tf_op jit(solution)/shard_map/all_to_all | solution.py:41
  278.7 3.9 %copy-start.2 = (bf16[2,128,3584]{1,2,0:T(8,128)(2,1)S(1)}, bf16[2,128,3584]{1,2,0:T(8,128)(2,1)}, u32[]{:S(2)}) copy-start(bf16[2,128,3584]{1,2,0:T(8,128)(2,1)} %copy.70) | copy-start | bytes 5505028
  282.6 1.5 copy-start.4
  284.9 1.5 copy-start.4
  290.9 22.9 %all-to-all-start.5 = ((bf16[2,128,256]{2,0,1:T(2,128)(2,1)}), bf16[2,128,256]{2,0,1:T(2,128)(2,1)S(1)}, u32[]{:S(2)}, u32[]{:S(2)}) async-start(bf16[2,128,256]{2,0,1:T(2,128)(2,1)} %copy.72), calls=%async_computation.5 | async-start | bytes 262144 | tf_op jit(solution)/shard_map/all_to_all | solution.py:41
where the time goes:
time: 317 us; the launch traced here: 315 us
  waiting for transfers between devices  176 us (56%)
  starting transfers between devices  62.7 us (20%)
  local copies, waits for them, and re-layouts  54.2 us (17%)
  blocking collectives  10.5 us (3%)
  other arithmetic  5.92 us (2%)
    all_to_all x2, waiting for transfers between devices, shards(): lax.all_to_all(send_buffer, 'ep', split_axis=1, concat_axis=1, tiled=True)  83.6 us
    all_to_all x1, waiting for transfers between devices, shards(): lax.all_to_all(pieces, 'ep', split_axis=0, concat_axis=0, tiled=True)  44.2 us
    all_to_all x1, waiting for transfers between devices, shards(): lax.all_to_all(jnp.take(lax.all_to_all(pieces, 'ep', split_axis=0, concat...  38.2 us
    all_to_all x2, starting transfers between devices, shards(): lax.all_to_all(send_buffer, 'ep', split_axis=1, concat_axis=1, tiled=True)  28.6 us
    all_to_all x2, starting transfers between devices, serve_rows(): lax.all_to_all(activated, 'ep', split_axis=1, concat_axis=1, tiled=True)  18.5 us
    while x5, local copies, waits for them, and re-layouts, serve_rows(): activated = lax.map(one_slot, arrived)  12.7 us
    all_gather x1, blocking collectives, shards(): grouped = lax.all_gather(tokens, 'dp', axis=1, tiled=True)  10.5 us
    all_to_all x2, waiting for transfers between devices, serve_rows(): lax.all_to_all(activated, 'ep', split_axis=1, concat_axis=1, tiled=True)  10.3 us
  transfers between devices with their start and end apart: 6, of which 6 were waited for; matrix products, arithmetic and copies ran while one was open for 13% of the time, Pallas kernels for 0%

commit v1 on v0

--- a/solution.py
+++ b/solution.py
@@ -74,7 +74,9 @@
     ).reshape(old_block.shape)
     first_serve = (new_block, new_expert)
     serve_plans = [first_serve] + [(new_block, new_expert)] * (tokens.shape[0] - 1)
-    grouped = lax.all_gather(tokens, "dp", axis=1, tiled=True)
+    grouped = jnp.concatenate(
+        lax.all_to_all(jnp.stack([tokens] * lax.axis_size("dp")), "dp", 0, 0), axis=1
+    )
     columns = grouped.shape[2]
     combined_steps = []
     for decode_step in range(tokens.shape[0]):

time: 317 us -> 306 us (0.965)
  blocking collectives: 10.5 us -> 0 us
  waiting for transfers between devices: 176 us -> 172 us
  starting transfers between devices: 62.7 us -> 66.4 us
    all_to_all x2, starting transfers between devices: 28.6 us -> 16.3 us  [shards(): lax.all_to_all(send_buffer, 'ep', split_axis=1, concat_axis=1, tiled=True)]
    all_to_all x1, starting transfers between devices: 7.79 us -> 19 us  [shards(): lax.all_to_all(pieces, 'ep', split_axis=0, concat_axis=0, tiled=True)]
    all_gather x1 -> x0, blocking collectives: 10.5 us -> none  [shards(): grouped = lax.all_gather(tokens, 'dp', axis=1, tiled=True)]
    all_to_all x0 -> x1, starting transfers between devices: none -> 4.83 us  [shards(): lax.all_to_all(jnp.stack([tokens] * lax.axis_size('dp')), 'dp', 0, 0)]
    all_to_all x2, waiting for transfers between devices: 83.6 us -> 79.1 us  [shards(): lax.all_to_all(send_buffer, 'ep', split_axis=1, concat_axis=1, tiled=True)]
  transfers between devices with their start and end apart: 6 -> 7, of which waited for: 6 -> 7; matrix products, arithmetic and copies ran while one was open for 13% -> 16% of each run, Pallas kernels for 0% -> 0%
where the time goes in v1:
time: 306 us; the launch traced here: 305 us
  waiting for transfers between devices  172 us (56%)
  starting transfers between devices  66.4 us (22%)
  local copies, waits for them, and re-layouts  55.1 us (18%)
  other arithmetic  5.19 us (2%)
    all_to_all x2, waiting for transfers between devices, shards(): lax.all_to_all(send_buffer, 'ep', split_axis=1, concat_axis=1, tiled=True)  79.1 us
    all_to_all x1, waiting for transfers between devices, shards(): lax.all_to_all(pieces, 'ep', split_axis=0, concat_axis=0, tiled=True)  42.8 us
    all_to_all x1, waiting for transfers between devices, shards(): lax.all_to_all(jnp.take(lax.all_to_all(pieces, 'ep', split_axis=0, concat...  38.2 us
    all_to_all x1, starting transfers between devices, shards(): lax.all_to_all(pieces, 'ep', split_axis=0, concat_axis=0, tiled=True)  19 us
    all_to_all x2, starting transfers between devices, serve_rows(): lax.all_to_all(activated, 'ep', split_axis=1, concat_axis=1, tiled=True)  18.5 us
    all_to_all x2, starting transfers between devices, shards(): lax.all_to_all(send_buffer, 'ep', split_axis=1, concat_axis=1, tiled=True)  16.3 us
    while x5, local copies, waits for them, and re-layouts, serve_rows(): activated = lax.map(one_slot, arrived)  12.7 us
    all_to_all x2, waiting for transfers between devices, serve_rows(): lax.all_to_all(activated, 'ep', split_axis=1, concat_axis=1, tiled=True)  10.3 us
  transfers between devices with their start and end apart: 7, of which 7 were waited for; matrix products, arithmetic and copies ran while one was open for 16% of the time, Pallas kernels for 0%

profile of v1, /device:TPU:1, one launch (start us, length us, event | category | flops | bytes accessed | tf_op | source)
XLA Modules:
  0.0 304.6 jit_solution(17442843662168395449)
XLA Ops:
  2.2 4.8 %all-to-all-start = ((bf16[4,2,4,3584]{3,2,1,0:T(4,128)(2,1)}), bf16[4,2,4,3584]{3,2,1,0:T(4,128)(2,1)S(1)}, u32[]{:S(2)}, u32[]{:S(2)}) async-start(bf16[4,2,4,3584]{3,2,1,0:T(4,128)(2,1)} %stack.4), calls=%async_computation | async-start | bytes 458752 | tf_op jit(solution)/shard_map/all_to_all | solution.py:78
  7.0 3.7 %reshape_squeeze.3 = bf16[128,28,256]{2,1,0:T(8,128)(2,1)} reshape(bf16[1,3584,256]{2,1,0:T(8,128)(2,1)} %param.14) | data formatting | bytes 3670016 | tf_op jit(solution)/shard_map/reshape;squeeze | solution.py:65
  12.4 19.0 %all-to-all-start.2 = ((bf16[128,28,256]{2,1,0:T(8,128)(2,1)}), bf16[128,28,256]{2,1,0:T(8,128)(2,1)S(1)}, u32[]{:S(2)}, u32[]{:S(2)}) async-start(bf16[128,28,256]{2,1,0:T(8,128)(2,1)} %reshape_squeeze.3), calls=%async_computation.2 | async-start | bytes 4194304 | tf_op jit(solution)/shard_map/all_to_all | solution.py:68
  32.9 3.3 %scatter_custom_fusion = bf16[256,3584]{1,0:T(8,128)(2,1)} fusion(s32[128]{0:T(128)S(1)} %get-tuple-element.130, bf16[]{:T(256)} %constant.58.clone.1, bf16[16,3584]{1,0:T(8,128)(2,1)S(1)} %squeeze.17), kind=kCustom, calls=%fused_computation.26 | custom fusion | bytes 1949698 | tf_op jit(solution)/shard_map/scatter | solution.py:87
  36.2 4.6 %copy.40 = bf16[2,128,3584]{2,0,1:T(2,128)(2,1)} copy(bf16[2,128,3584]{2,1,0:T(8,128)(2,1)} %bitcast.125) | data formatting | bytes 3670016 | tf_op jit(solution)/shard_map/reshape | solution.py:88
  40.8 42.8 %all-to-all-done.2 = bf16[128,28,256]{2,1,0:T(8,128)(2,1)S(1)} async-done(((bf16[128,28,256]{2,1,0:T(8,128)(2,1)}), bf16[128,28,256]{2,1,0:T(8,128)(2,1)S(1)}, u32[]{:S(2)}, u32[]{:S(2)}) %all-to-all-start.2) | async-done | bytes 1835040 | tf_op jit(solution)/shard_map/all_to_all | solution.py:68
  83.6 8.1 %all-to-all-start.1 = ((bf16[2,128,3584]{2,0,1:T(2,128)(2,1)}), bf16[2,128,3584]{2,0,1:T(2,128)(2,1)}, u32[]{:S(2)}, u32[]{:S(2)}) async-start(bf16[2,128,3584]{2,0,1:T(2,128)(2,1)} %copy.40), calls=%async_computation.1 | async-start | bytes 3670016 | tf_op jit(solution)/shard_map/all_to_all | solution.py:91
  91.7 3.3 %scatter_custom_fusion.1 = bf16[256,3584]{1,0:T(8,128)(2,1)} fusion(s32[128]{0:T(128)S(1)} %get-tuple-element.131, bf16[]{:T(256)} %constant.58.clone.1, bf16[16,3584]{1,0:T(8,128)(2,1)S(1)} %squeeze.20), kind=kCustom, calls=%fused_computation.24 | custom fusion | bytes 1949698 | tf_op jit(solution)/shard_map/scatter | solution.py:87
  95.1 4.6 %copy.48 = bf16[2,128,3584]{2,0,1:T(2,128)(2,1)} copy(bf16[2,128,3584]{2,1,0:T(8,128)(2,1)} %bitcast.126) | data formatting | bytes 3670016 | tf_op jit(solution)/shard_map/reshape | solution.py:88
  99.7 38.2 %all-to-all-done.1 = bf16[2,128,3584]{2,0,1:T(2,128)(2,1)} async-done(((bf16[2,128,3584]{2,0,1:T(2,128)(2,1)}), bf16[2,128,3584]{2,0,1:T(2,128)(2,1)}, u32[]{:S(2)}, u32[]{:S(2)}) %all-to-all-start.1) | async-done | bytes 1835040 | tf_op jit(solution)/shard_map/all_to_all | solution.py:91
  137.9 8.2 %all-to-all-start.5 = ((bf16[2,128,3584]{2,0,1:T(2,128)(2,1)}), bf16[2,128,3584]{2,0,1:T(2,128)(2,1)}, u32[]{:S(2)}, u32[]{:S(2)}) async-start(bf16[2,128,3584]{2,0,1:T(2,128)(2,1)} %copy.48), calls=%async_computation.5 | async-start | bytes 3670016 | tf_op jit(solution)/shard_map/all_to_all | solution.py:91
  148.2 3.2 %broadcast_select_fusion = bf16[128,28,256]{2,1,0:T(8,128)(2,1)} fusion(bf16[128,28,256]{2,1,0:T(8,128)(2,1)} %gather_fusion, pred[128]{0:T(512)(128)(4,1)S(1)} %compare_and_fusion), kind=kLoop, calls=%fused_computation.23 | loop fusion | flops 917504 | bytes 3670144 | tf_op jit(solution)/shard_map/jit(_take)/select_n | solution.py:67
  151.4 40.9 %all-to-all-done.5 = bf16[2,128,3584]{2,0,1:T(2,128)(2,1)} async-done(((bf16[2,128,3584]{2,0,1:T(2,128)(2,1)}), bf16[2,128,3584]{2,0,1:T(2,128)(2,1)}, u32[]{:S(2)}, u32[]{:S(2)}) %all-to-all-start.5) | async-done | bytes 1835040 | tf_op jit(solution)/shard_map/all_to_all | solution.py:91
  192.3 7.8 %all-to-all-start.3 = ((bf16[128,28,256]{2,1,0:T(8,128)(2,1)}), bf16[128,28,256]{2,1,0:T(8,128)(2,1)S(1)}, u32[]{:S(2)}, u32[]{:S(2)}) async-start(bf16[128,28,256]{2,1,0:T(8,128)(2,1)} %broadcast_select_fusion), calls=%async_computation.3 | async-start | bytes 4194304 | tf_op jit(solution)/shard_map/all_to_all | solution.py:66
  202.9 5.6 %copy.42 = bf16[2,128,3584]{1,2,0:T(8,128)(2,1)} copy(bf16[2,128,3584]{2,0,1:T(2,128)(2,1)} %all-to-all-done.1) | data formatting | bytes 3670016 | tf_op jit(solution)/shard_map/while | solution.py:40
  208.5 5.5 %copy.49 = bf16[2,128,3584]{1,2,0:T(8,128)(2,1)} copy(bf16[2,128,3584]{2,0,1:T(2,128)(2,1)} %all-to-all-done.5) | data formatting | bytes 3670016 | tf_op jit(solution)/shard_map/while | solution.py:40
  214.0 38.2 %all-to-all-done.3 = bf16[128,28,256]{2,1,0:T(8,128)(2,1)S(1)} async-done(((bf16[128,28,256]{2,1,0:T(8,128)(2,1)}), bf16[128,28,256]{2,1,0:T(8,128)(2,1)S(1)}, u32[]{:S(2)}, u32[]{:S(2)}) %all-to-all-start.3) | async-done | bytes 1835040 | tf_op jit(solution)/shard_map/all_to_all | solution.py:66
  254.1 5.2 %while.22 = (s32[]{:T(128)}, bf16[2,128,256]{2,1,0:T(8,128)(2,1)S(1)}, bf16[2,128,3584]{1,2,0:T(8,128)(2,1)}, bf16[128,28,256]{2,1,0:T(8,128)(2,1)}, f32[28,2]{1...) while((s32[]{:T(128)}, bf16[2,128,256]{2,1,0:T(8,128)(2,1)S(1)}, ...), condition=%wide.wide.region_8.9_spmd, body=%wide.wide.region_6.8_spmd.sunk | while | flops 236847104 | bytes 12439901 | solution.py:40
  260.1 7.7 %all-to-all-start.4 = ((bf16[2,128,256]{2,0,1:T(2,128)(2,1)}), bf16[2,128,256]{2,0,1:T(2,128)(2,1)S(1)}, u32[]{:S(2)}, u32[]{:S(2)}) async-start(bf16[2,128,256]{2,0,1:T(2,128)(2,1)} %copy.44), calls=%async_computation.4 | async-start | bytes 262144 | tf_op jit(solution)/shard_map/all_to_all | solution.py:41
  267.8 3.9 %reshape_reshape.8 = bf16[28,128,256]{2,1,0:T(8,128)(2,1)} reshape(bf16[128,28,256]{2,1,0:T(8,128)(2,1)} %get-tuple-element.295) | data formatting | bytes 3670016 | tf_op jit(solution)/shard_map/while/body/eval_jaxpr/reshape;reshape | solution.py:26
  271.7 4.6 %while.23 = (s32[]{:T(128)}, bf16[2,128,256]{2,1,0:T(8,128)(2,1)S(1)}, bf16[2,128,3584]{1,2,0:T(8,128)(2,1)S(1)}, bf16[128,28,256]{2,1,0:T(8,128)(2,1)}, f32[28,...) while((s32[]{:T(128)}, bf16[2,128,256]{2,1,0:T(8,128)(2,1)S(1)}, ...), condition=%wide.wide.region_16.17_spmd, body=%wide.wide.region_14.16_spmd.sunk | while | flops 236847104 | bytes 12439901 | solution.py:40
  280.1 10.8 %all-to-all-start.6 = ((bf16[2,128,256]{2,0,1:T(2,128)(2,1)}), bf16[2,128,256]{2,0,1:T(2,128)(2,1)S(1)}, u32[]{:S(2)}, u32[]{:S(2)}) async-start(bf16[2,128,256]{2,0,1:T(2,128)(2,1)} %copy.51), calls=%async_computation.6 | async-start | bytes 262144 | tf_op jit(solution)/shard_map/all_to_all | solution.py:41
  291.0 3.7 %broadcast_in_dim_reshape.3 = bf16[1,3584,256]{2,1,0:T(8,128)(2,1)} reshape(bf16[128,28,256]{2,1,0:T(8,128)(2,1)} %get-tuple-element.296) | data formatting | bytes 3670016 | tf_op jit(solution)/shard_map/broadcast_in_dim;reshape | solution.py:97
  295.7 7.3 %all-to-all-done.6 = bf16[2,128,256]{2,0,1:T(2,128)(2,1)S(1)} async-done(((bf16[2,128,256]{2,0,1:T(2,128)(2,1)}), bf16[2,128,256]{2,0,1:T(2,128)(2,1)S(1)}, u32[]{:S(2)}, u32[]{:S(2)}) %all-to-all-start.6) | async-done | bytes 131104 | tf_op jit(solution)/shard_map/all_to_all | solution.py:41
  (89 shorter events, 26.2 us)
Async XLA Ops:
  0.6 202.0 %copy-start = (f32[128,28,2]{0,2,1:T(2,128)S(1)}, f32[128,28,2]{0,2,1:T(2,128)}, u32[]{:S(2)}) copy-start(f32[128,28,2]{0,2,1:T(2,128)} %param.15) | copy-start | bytes 86020
  2.2 10.2 %all-to-all-start = ((bf16[4,2,4,3584]{3,2,1,0:T(4,128)(2,1)}), bf16[4,2,4,3584]{3,2,1,0:T(4,128)(2,1)S(1)}, u32[]{:S(2)}, u32[]{:S(2)}) async-start(bf16[4,2,4,3584]{3,2,1,0:T(4,128)(2,1)} %stack.4), calls=%async_computation | async-start | bytes 458752 | tf_op jit(solution)/shard_map/all_to_all | solution.py:78
  10.8 20.6 %copy-start.5 = (s32[2,16,8]{1,2,0:T(8,128)S(1)}, s32[2,16,8]{1,2,0:T(8,128)}, u32[]{:S(2)}) copy-start(s32[2,16,8]{1,2,0:T(8,128)} %param.12) | copy-start | bytes 3076
  10.8 21.5 %copy-start.7 = (s32[128]{0:T(128)S(1)}, s32[128]{0:T(128)}, u32[]{:S(2)}) copy-start(s32[128]{0:T(128)} %param.17) | copy-start | bytes 1540
  10.8 21.5 %copy-start.8 = (s32[128]{0:T(128)S(1)}, s32[128]{0:T(128)}, u32[]{:S(2)}) copy-start(s32[128]{0:T(128)} %param.16) | copy-start | bytes 1540
  12.4 71.2 %all-to-all-start.2 = ((bf16[128,28,256]{2,1,0:T(8,128)(2,1)}), bf16[128,28,256]{2,1,0:T(8,128)(2,1)S(1)}, u32[]{:S(2)}, u32[]{:S(2)}) async-start(bf16[128,28,256]{2,1,0:T(8,128)(2,1)} %reshape_squeeze.3), calls=%async_computation.2 | async-start | bytes 4194304 | tf_op jit(solution)/shard_map/all_to_all | solution.py:68
  83.6 54.3 %all-to-all-start.1 = ((bf16[2,128,3584]{2,0,1:T(2,128)(2,1)}), bf16[2,128,3584]{2,0,1:T(2,128)(2,1)}, u32[]{:S(2)}, u32[]{:S(2)}) async-start(bf16[2,128,3584]{2,0,1:T(2,128)(2,1)} %copy.40), calls=%async_computation.1 | async-start | bytes 3670016 | tf_op jit(solution)/shard_map/all_to_all | solution.py:91
  137.9 54.4 %all-to-all-start.5 = ((bf16[2,128,3584]{2,0,1:T(2,128)(2,1)}), bf16[2,128,3584]{2,0,1:T(2,128)(2,1)}, u32[]{:S(2)}, u32[]{:S(2)}) async-start(bf16[2,128,3584]{2,0,1:T(2,128)(2,1)} %copy.48), calls=%async_computation.5 | async-start | bytes 3670016 | tf_op jit(solution)/shard_map/all_to_all | solution.py:91
  151.4 51.5 %copy-start.6 = (f32[2,16,8]{1,2,0:T(8,128)S(1)}, f32[2,16,8]{1,2,0:T(8,128)}, u32[]{:S(2)}) copy-start(f32[2,16,8]{1,2,0:T(8,128)} %param.13) | copy-start | bytes 3076
  192.3 59.9 %all-to-all-start.3 = ((bf16[128,28,256]{2,1,0:T(8,128)(2,1)}), bf16[128,28,256]{2,1,0:T(8,128)(2,1)S(1)}, u32[]{:S(2)}, u32[]{:S(2)}) async-start(bf16[128,28,256]{2,1,0:T(8,128)(2,1)} %broadcast_select_fusion), calls=%async_computation.3 | async-start | bytes 4194304 | tf_op jit(solution)/shard_map/all_to_all | solution.py:66
  252.2 1.9 copy-start.1
  254.1 1.8 copy-start.4
  256.7 1.8 copy-start.4
  260.1 20.0 %all-to-all-start.4 = ((bf16[2,128,256]{2,0,1:T(2,128)(2,1)}), bf16[2,128,256]{2,0,1:T(2,128)(2,1)S(1)}, u32[]{:S(2)}, u32[]{:S(2)}) async-start(bf16[2,128,256]{2,0,1:T(2,128)(2,1)} %copy.44), calls=%async_computation.4 | async-start | bytes 262144 | tf_op jit(solution)/shard_map/all_to_all | solution.py:41
  267.8 3.9 %copy-start.2 = (bf16[2,128,3584]{1,2,0:T(8,128)(2,1)S(1)}, bf16[2,128,3584]{1,2,0:T(8,128)(2,1)}, u32[]{:S(2)}) copy-start(bf16[2,128,3584]{1,2,0:T(8,128)(2,1)} %copy.49) | copy-start | bytes 5505028
  271.7 1.5 copy-start.3
  274.0 1.5 copy-start.3
  280.1 22.9 %all-to-all-start.6 = ((bf16[2,128,256]{2,0,1:T(2,128)(2,1)}), bf16[2,128,256]{2,0,1:T(2,128)(2,1)S(1)}, u32[]{:S(2)}, u32[]{:S(2)}) async-start(bf16[2,128,256]{2,0,1:T(2,128)(2,1)} %copy.51), calls=%async_computation.6 | async-start | bytes 262144 | tf_op jit(solution)/shard_map/all_to_all | solution.py:41
